TPU v7x, 256 devices: a whole 4x4x8 slice. The times are simulated.
256 devices in a mesh: sect: 2 (over y_lo), batch: 16 (over z, core), head: 8 (over x, y_hi).
Axes of the slice: x: 4, y: 4 (y_hi: 2, y_lo: 2; y = y_hi * 2 + y_lo), z: 8, core: 2. Of those that a mesh axis runs over, the one named last changes fastest.
Arguments:
- queries: bfloat16 [96, 16, 512], P('batch', 'head', 'sect'), may hold values from -51 to 51
- newest_key_value: bfloat16 [96, 4, 256], P('batch'), may hold values from -5 to 5
- page_cache: bfloat16 [96, 256, 64, 256], P('batch', ('sect', 'head')), may hold values from -4 to 4
- lengths: int32 [96], P('batch'), may hold values from 2048 to 4096, as said below
- page_ids: int32 [96, 4, 32], P('batch'), may hold values from 0 to 63, as said below
- out_weight: bfloat16 [8192, 4096], P(('sect', 'head'), 'batch'), may hold values from -0.0625 to 0.0625
- residual: bfloat16 [96, 4096], P(None, 'batch'), may hold values from -2 to 2
- norm_gain: float32 [4096], P('batch'), may hold values from 0.25 to 1.75
- expert_ids: int32 [96, 8], replicated, may hold values from 0 to 63, all different within a row; in each aligned block of 96 rows (0 to 95, 96 to 191, ...) at most 24 rows name the same one
- route_weight: float32 [96, 8], replicated, may hold values from 0.1 to 1
- gate_up_weight: bfloat16 [32, 4096, 2, 3072], P(('sect', 'batch'), None, None, 'head'), may hold values from -0.09375 to 0.09375
- down_weight: bfloat16 [32, 3072, 4096], P(('sect', 'batch'), 'head'), may hold values from -0.15625 to 0.15625
Outputs:
- layer_out: bfloat16 [96, 4096], P(None, 'batch')
Inputs may be any that keep to these rules, and one draw needn't show every extreme that they name: `lengths`: some sequence holds exactly 4096 cached tokens and some exactly 2048. `page_ids`: each row lists 32 different pages in ascending order, all below the number of pages that hold the sequence's cached tokens, and always the last of those pages. `expert_ids`: each row names 8 different experts; over all rows no expert is named by more than 24 rows, a bound that some block reaches.
All inputs are finite; a program needn't handle non-finite values.
Results may differ from a plain program's by a relative error of at most 0.025.
Values may be sent and summed in bfloat16 or wider, within the bound.
No kernel may reach another device: no remote copies, remote signals or barrier semaphores. Data moves between devices by JAX's collectives and lax.ppermute only.
A program may use at most 128 MiB of HBM per device.

v0:
```python
import math
import jax
import jax.numpy as jnp
from jax import lax
from jax.sharding import PartitionSpec as P

D = 4096
EXPERTS = 64
NEG_FILL = -1e30
NORM_EPS = 1e-06


def copy_for_each(shard, axis):
    copies = jnp.broadcast_to(shard, (lax.axis_size(axis), *shard.shape))
    return lax.all_to_all(copies, axis, split_axis=0, concat_axis=0, tiled=True)


def in_order(pieces, dim):
    lengths = list(pieces.shape[1:])
    lengths[dim] *= pieces.shape[0]
    return jnp.moveaxis(pieces, 0, dim).reshape(lengths)


def gathered_copies(shard, axis, dim):
    pieces = copy_for_each(shard, axis)
    return in_order(pieces, dim)


def from_partner(shard, axis, distance):
    return lax.ppermute(shard, axis, [(i, i ^ 1 << distance) for i in range(lax.axis_size(axis))])


def taken_together(shard, axis):
    return copy_for_each(shard, axis).astype(jnp.float32).sum(axis=0)


def of_everyone(shard, axis):
    return copy_for_each(shard, axis).sum(axis=0)


def merge_pair(first, second):
    first_max, first_sum, first_acc = first
    second_max, second_sum, second_acc = second
    joined = jnp.maximum(first_max, second_max)
    first_factor = jnp.exp(first_max - joined)
    second_factor = jnp.exp(second_max - joined)
    return (
        joined,
        first_sum * first_factor + second_sum * second_factor,
        first_acc * first_factor[..., None] + second_acc * second_factor[..., None],
    )


def head_slice(partial_value, begin_at, span_size):
    return tuple(
        (lax.dynamic_slice_in_dim(member, begin_at, span_size, 1) for member in partial_value)
    )


def on_device(
    queries,
    newest_key_value,
    page_cache,
    lengths,
    page_ids,
    out_weight,
    residual,
    norm_gain,
    expert_ids,
    route_weight,
    gate_up_weight,
    down_weight,
):
    seq_count = queries.shape[0]
    head_dim = newest_key_value.shape[2] // 2
    kv_heads = newest_key_value.shape[1]
    sect_size = lax.axis_size("sect")
    head_size = lax.axis_size("head")
    batch_size = lax.axis_size("batch")
    group_size = sect_size * head_size // kv_heads
    position = lax.axis_index("sect") * head_size + lax.axis_index("head")
    kv_index = position // group_size
    quarter = position % group_size
    local_pages = page_cache.shape[1]
    page_len = page_cache.shape[2]
    scaling = 1.0 / math.sqrt(head_dim)
    all_heads = lax.all_gather(queries, "head", axis=1, tiled=True)
    kv_local = kv_index % (kv_heads // sect_size)
    group_query = lax.dynamic_slice_in_dim(all_heads, kv_local * head_dim, head_dim, 2)
    heads_dev = all_heads.shape[1] // group_size
    block_cols = heads_dev * head_dim
    chosen = lax.dynamic_index_in_dim(page_ids, kv_index, 1, keepdims=False)
    leading_page = quarter * local_pages
    page_number = jnp.broadcast_to(
        leading_page + jnp.arange(local_pages, dtype=jnp.int32), (seq_count, local_pages)
    )
    page_used = jnp.any(chosen[:, :, None] == page_number[:, None, :], axis=1)
    token_place = (
        page_number[:, :, None] * page_len + jnp.arange(page_len, dtype=jnp.int32)[None, None, :]
    )
    key_count = page_cache.shape[1] * page_len
    usable_pages = (page_used[:, :, None] & (token_place < lengths[:, None, None])).reshape(
        seq_count, key_count
    )
    gathered_keys = page_cache[..., :head_dim].reshape(seq_count, key_count, head_dim)
    gathered_values = page_cache[..., head_dim:].reshape(seq_count, key_count, head_dim)
    scores = (
        jnp.einsum("shd,skd->shk", group_query, gathered_keys, preferred_element_type=jnp.float32)
        * scaling
    )
    scores = jnp.where(usable_pages[:, None, :], scores, NEG_FILL)
    newest_entry = lax.dynamic_index_in_dim(newest_key_value, kv_index, 1, keepdims=False)
    fresh_score = (
        jnp.einsum(
            "shd,sd->sh",
            group_query,
            newest_entry[:, :head_dim],
            preferred_element_type=jnp.float32,
        )
        * scaling
    )
    leading = quarter == 0
    fresh_score = jnp.where(leading, fresh_score, NEG_FILL)
    running_max = jnp.maximum(jnp.max(scores, axis=2), fresh_score)
    weights = jnp.where(usable_pages[:, None, :], jnp.exp(scores - running_max[..., None]), 0.0)
    fresh_weight = jnp.where(leading, jnp.exp(fresh_score - running_max), 0.0)
    running_sum = jnp.sum(weights, axis=2) + fresh_weight
    weighted = jnp.einsum(
        "shk,skd->shd",
        weights.astype(jnp.bfloat16),
        gathered_values,
        preferred_element_type=jnp.float32,
    )
    weighted = weighted + fresh_weight.astype(jnp.bfloat16).astype(jnp.float32)[
        ..., None
    ] * newest_entry[:, None, head_dim:].astype(jnp.float32)
    partial_value = (running_max, running_sum, weighted)
    bit_count = group_size.bit_length() - 1
    for bit_index in reversed(range(bit_count)):
        half_heads = partial_value[0].shape[1] // 2
        keep_half = quarter >> bit_index & 1
        kept = head_slice(partial_value, keep_half * half_heads, half_heads)
        sent = head_slice(partial_value, (1 - keep_half) * half_heads, half_heads)
        partner = from_partner(sent, "head", bit_index)
        partial_value = merge_pair(kept, partner)
    attention = (
        (partial_value[2] / partial_value[1][..., None])
        .reshape(seq_count, block_cols)
        .astype(jnp.bfloat16)
    )
    head_terms = jnp.dot(
        lax.all_gather(attention, "batch", axis=0, tiled=True),
        out_weight,
        preferred_element_type=jnp.float32,
    )
    projected = lax.psum(head_terms, ("sect", "head"))
    hidden_state = residual.astype(jnp.float32) + projected
    squares = lax.psum(jnp.sum(hidden_state * hidden_state, axis=1), "batch")
    inverse = lax.rsqrt(squares / D + NORM_EPS)
    normed = (hidden_state * inverse[:, None] * norm_gain[None, :]).astype(jnp.bfloat16)
    token_count, top_count = expert_ids.shape
    capacity = 2 * token_count * top_count // EXPERTS
    pair_local = gate_up_weight.shape[0]
    flat_ids = expert_ids.reshape(-1)
    one_hot = (flat_ids[:, None] == jnp.arange(EXPERTS, dtype=jnp.int32)[None, :]).astype(jnp.int32)
    earlier = jnp.cumsum(one_hot, axis=0) - one_hot
    rank_in = jnp.sum(earlier * one_hot, axis=1)
    sub_half = lax.axis_index("head") // (head_size // 2)
    pair_first = lax.axis_index("sect") * (batch_size * pair_local)
    local_pair = flat_ids // 2 - pair_first
    in_sect = (local_pair >= 0) & (local_pair < batch_size * pair_local)
    full_slot = (
        (local_pair // pair_local * 2 + flat_ids % 2) * pair_local + local_pair % pair_local
    ) * capacity + rank_in
    full_slot = jnp.where(in_sect, full_slot, -1)
    slot_dev = pair_local * capacity
    slot_total = batch_size * 2 * slot_dev
    send_count = batch_size * slot_dev
    matches = (
        full_slot.reshape(token_count, top_count)[None, :, :]
        == jnp.arange(slot_total, dtype=jnp.int32)[:, None, None]
    )
    selector_full = (
        jnp.any(matches, axis=2).astype(jnp.bfloat16).reshape(batch_size, 2, slot_dev, token_count)
    )
    selector = lax.dynamic_index_in_dim(selector_full, sub_half, 1, keepdims=False).reshape(
        send_count, token_count
    )
    coefficient = route_weight / jnp.sum(route_weight, axis=1, keepdims=True)
    combine_full = jnp.sum(jnp.where(matches, coefficient[None, :, :], 0.0), axis=2).T
    cols_dev = normed.shape[1]
    outgoing = jnp.dot(selector, normed, preferred_element_type=jnp.float32).astype(jnp.bfloat16)
    outgoing = outgoing.reshape(batch_size, pair_local, capacity, cols_dev)
    arrived = lax.all_to_all(outgoing, "batch", split_axis=0, concat_axis=3, tiled=True)[0]
    mixture = jnp.einsum(
        "ecd,edgf->ecgf", arrived, gate_up_weight, preferred_element_type=jnp.float32
    )
    activated = (jax.nn.silu(mixture[:, :, 0]) * mixture[:, :, 1]).astype(jnp.bfloat16)
    expert_part = jnp.einsum(
        "ecf,efd->ecd", activated, down_weight, preferred_element_type=jnp.float32
    )
    leaving = expert_part.reshape(1, slot_dev, batch_size, cols_dev)
    came_back = (
        lax.all_to_all(
            leaving.astype(jnp.bfloat16), "batch", split_axis=2, concat_axis=0, tiled=True
        )
        .astype(leaving.dtype)
        .reshape(send_count, cols_dev)
    )
    weights_used = lax.dynamic_index_in_dim(
        combine_full.reshape(token_count, batch_size, 2, slot_dev), sub_half, 2, keepdims=False
    )
    weights_used = weights_used.reshape(token_count, send_count)
    combined = jnp.dot(weights_used, came_back, preferred_element_type=jnp.float32)
    expert_mix = lax.psum(combined, ("sect", "head"))
    return (hidden_state + expert_mix).astype(jnp.bfloat16)


def solution(mesh):
    placed = (
        P("batch", "head", "sect"),
        P("batch", None, None),
        P("batch", ("sect", "head"), None, None),
        P("batch"),
        P("batch", None, None),
        P(("sect", "head"), "batch"),
        P(None, "batch"),
        P("batch"),
        P(),
        P(),
        P(("sect", "batch"), None, None, "head"),
        P(("sect", "batch"), "head", None),
    )
    return jax.shard_map(
        on_device, mesh=mesh, in_specs=placed, out_specs=P(None, "batch"), check_vma=False
    )
```

profile of v0, /device:TPU:32, one launch (start us, length us, event | category | flops | bytes accessed | tf_op | source)
XLA Modules:
  0.0 342.4 jit_solution(5951458100370429770)
XLA Ops:
  6.5 0.7 copy.66
  7.3 34.3 %all_gather.6 = bf16[6,16,256]{2,0,1:T(8,128)(2,1)S(1)} all-gather(bf16[6,2,256]{2,0,1:T(8,128)(2,1)S(1)} %copy.66), channel_id=1, replica_groups=mesh['sect'=2,'batch'=16,'head'=8] {'head'}, dimensions={1}, use_global_device_ids=true | all-gather | bytes 55296 | tf_op jit(solution)/shard_map/all_gather | solution.py:87
  41.6 0.7 constant_dynamic-slice_fusion.14
  42.3 0.2 compare_reduce_fusion
  42.5 0.1 and.72
  42.6 0.1 and.73
  42.7 0.1 iota_add_fusion
  42.8 0.1 add.157
  42.9 3.2 fusion.49
  46.2 0.1 fusion.29
  46.3 0.1 compare_and_fusion
  46.4 1.3 fusion.50
  47.7 0.1 constant_dynamic-slice_fusion.10
  47.7 0.0 collective-permute-start
  47.8 1.2 fusion.8
  49.0 0.1 constant_dynamic-slice_fusion.4
  49.1 2.0 collective-permute-start.4
  51.1 1.4 convolution_add_fusion
  52.5 0.1 collective-permute-start.1
  52.7 0.1 copy.69
  52.7 0.1 eq.65
  52.8 0.1 eq.61
  53.0 1.8 reduce-window.6
  54.8 0.3 slice_reduce_fusion
  55.1 0.1 fusion.13
  55.2 0.1 reduce_sum.49
  55.3 0.1 fusion.22
  55.4 0.8 fusion.2
  56.2 0.2 copy.78
  56.4 0.1 fusion.34
  56.5 0.1 constant_dynamic-slice_fusion.7
  56.6 3.2 collective-permute-start.2
  59.8 0.1 constant_dynamic-slice_fusion.2
  59.9 0.3 collective-permute-start.5
  60.2 0.1 multiply_add_fusion
  60.3 3.3 collective-permute-start.3
  63.6 1.4 collective-permute-done.5
  65.0 0.1 fusion.36
  65.0 0.5 collective-permute-done.3
  65.6 0.1 fusion.32
  65.7 18.2 %all-gather = bf16[16,6,512]{2,1,0:T(8,128)(2,1)S(1)} all-gather(bf16[1,6,512]{2,1,0:T(8,128)(2,1)S(1)} %reshape.182), channel_id=1, replica_groups=mesh['sect'=2,'batch'=16,'head'=8] {'batch'}, dimensions={0}, use_global_device_ids=true | all-gather | bytes 104448 | tf_op jit(solution)/shard_map/all_gather | solution.py:152
  83.9 0.8 fusion.51
  84.8 94.1 %all-reduce.3.cloned.1.call-done = f32[96,256]{1,0:T(8,128)} async-done(((f32[96,256]{1,0:T(8,128)}), f32[96,256]{1,0:T(8,128)}) %all-reduce.3.cloned.1.call-update) | async-done | bytes 98320 | tf_op jit(solution)/shard_map/psum | solution.py:156
  178.9 1.0 multiply_reduce_fusion
  180.0 21.5 %psum.22 = f32[96]{0:T(128)S(1)} all-reduce(f32[96]{0:T(128)S(1)} %multiply_reduce_fusion), channel_id=1, replica_groups=mesh['sect'=2,'batch'=16,'head'=8] {'batch'}, use_global_device_ids=true, to_apply=%region_11.12 | all-reduce | flops 96 | bytes 768 | tf_op jit(solution)/shard_map/psum | solution.py:158
  201.4 1.8 convolution_convert_fusion.1
  203.3 9.6 %all-to-all-start = ((bf16[16,1,24,256]{3,2,1,0:T(8,128)(2,1)}), bf16[16,1,24,256]{3,2,1,0:T(8,128)(2,1)}, u32[]{:S(2)}, u32[]{:S(2)}) async-start(bf16[16,1,24,256]{3,2,1,0:T(8,128)(2,1)} %bitcast.13), calls=%async_computation | async-start | bytes 393216 | tf_op jit(solution)/shard_map/all_to_all | solution.py:194
  212.9 3.4 %copy.86 = bf16[4096,384]{1,0:T(8,128)(2,1)S(1)} copy(bf16[4096,384]{0,1:T(8,128)(2,1)} %bitcast.92) | data formatting | bytes 6291456 | tf_op jit(solution)/shard_map/ecf,efd->ecd/dot_general | solution.py:199
  216.3 0.6 reduce_sum.50
  216.9 4.6 %all-to-all-done = bf16[16,1,24,256]{3,2,1,0:T(8,128)(2,1)} async-done(((bf16[16,1,24,256]{3,2,1,0:T(8,128)(2,1)}), bf16[16,1,24,256]{3,2,1,0:T(8,128)(2,1)}, u32[]{:S(2)}, u32[]{:S(2)}) %all-to-all-start) | async-done | bytes 196640 | tf_op jit(solution)/shard_map/all_to_all | solution.py:194
  221.5 1.6 copy.80
  223.1 1.7 reshape.187
  224.8 3.8 %fusion.5 = f32[1,24,2,384]{3,1,2,0:T(8,128)S(1)} fusion(bf16[24,4096,1]{1,0,2:T(8,128)(2,1)} %reshape.187, bf16[4096,2,384]{2,1,0:T(2,128)(2,1)} %bitcast.102), kind=kOutput, calls=%fused_computation.10 | convolution fusion | flops 150994944 | bytes 6561792 | tf_op jit(solution)/shard_map/ecd,edgf->ecgf/dot_general | solution.py:195
  228.7 1.9 fusion.4
  230.6 4.8 %all-to-all-start.1 = ((bf16[1,24,16,256]{3,1,0,2:T(8,128)(2,1)}), bf16[1,24,16,256]{3,1,0,2:T(8,128)(2,1)S(1)}, u32[]{:S(2)}, u32[]{:S(2)}) async-start(bf16[1,24,16,256]{3,1,0,2:T(8,128)(2,1)} %fusion.4), calls=%async_computation.1 | async-start | bytes 393216 | tf_op jit(solution)/shard_map/all_to_all | solution.py:204
  235.3 0.0 all-reduce.5.cloned.1.call-start
  235.4 0.7 broadcast_divide_fusion
  236.1 0.1 copy.76
  236.2 1.6 select_reduce_fusion
  237.8 0.2 copy.77
  238.0 5.8 %all-to-all-done.1 = bf16[1,24,16,256]{3,1,0,2:T(8,128)(2,1)S(1)} async-done(((bf16[1,24,16,256]{3,1,0,2:T(8,128)(2,1)}), bf16[1,24,16,256]{3,1,0,2:T(8,128)(2,1)S(1)}, u32[]{:S(2)}, u32[]{:S(2)}) %all-to-all-start.1) | async-done | bytes 196640 | tf_op jit(solution)/shard_map/all_to_all | solution.py:204
  243.8 0.8 fusion.52
  244.7 89.4 %all-reduce.5.cloned.1.call-done = f32[96,256]{1,0:T(8,128)} async-done(((f32[96,256]{1,0:T(8,128)}), f32[96,256]{1,0:T(8,128)}) %all-reduce.5.cloned.1.call-update) | async-done | bytes 98320 | tf_op jit(solution)/shard_map/psum | solution.py:215
  334.0 1.5 add_convert_fusion
  (42 shorter events, 0.3 us)
Async XLA Ops:
  6.5 77.4 %copy-start = (bf16[512,256]{1,0:T(8,128)(2,1)S(1)}, bf16[512,256]{1,0:T(8,128)(2,1)}, u32[]{:S(2)}) copy-start(bf16[512,256]{1,0:T(8,128)(2,1)} %param.17) | copy-start | bytes 786436
  6.5 172.4 %all-reduce.3.cloned.1.call-start = ((), (), s32[]{:S(2)}) async-start(), calls=%async_computation.2 | async-start | bytes 196608 | tf_op jit(solution)/shard_map/psum | solution.py:156
  42.9 3.2 copy-start.6
  42.9 3.4 %copy-start.8 = (s32[6]{0:T(128)S(1)}, s32[6]{0:T(128)}, u32[]{:S(2)}) copy-start(s32[6]{0:T(128)} %param.15) | copy-start | bytes 76
  46.2 6.5 %copy-start.5 = (s32[96,8]{0,1:T(8,128)S(1)}, s32[96,8]{0,1:T(8,128)}, u32[]{:S(2)}) copy-start(s32[96,8]{0,1:T(8,128)} %param.20) | copy-start | bytes 9220
  47.7 8.7 %collective-permute-start = (f32[6,8]{1,0:T(8,128)S(1)}, f32[6,8]{1,0:T(8,128)S(1)}, u32[]{:S(2)}, u32[]{:S(2)}) collective-permute-start(f32[6,8]{1,0:T(8,128)S(1)} %constant_dynamic-slice_fusion.10), channel_id=1, source_target_pairs={{0,2},{1,3},{2,0},{3,1},{4,6},{5,7},{6,4},{7,5},{8,10},{9,11},{10,... | collective-permute-start | bytes 584 | tf_op jit(solution)/shard_map/ppermute | solution.py:30
  49.1 7.3 %collective-permute-start.4 = (f32[6,8]{1,0:T(8,128)S(1)}, f32[6,8]{1,0:T(8,128)S(1)}, u32[]{:S(2)}, u32[]{:S(2)}) collective-permute-start(f32[6,8]{1,0:T(8,128)S(1)} %constant_dynamic-slice_fusion.4), channel_id=1, source_target_pairs={{0,2},{1,3},{2,0},{3,1},{4,6},{5,7},{6,4},{7,5},{8,10},{9,11},{10,... | collective-permute-start | bytes 584 | tf_op jit(solution)/shard_map/ppermute | solution.py:30
  51.1 127.8 %copy-start.2 = (bf16[96,256]{1,0:T(8,128)(2,1)S(1)}, bf16[96,256]{1,0:T(8,128)(2,1)}, u32[]{:S(2)}) copy-start(bf16[96,256]{1,0:T(8,128)(2,1)} %param.18) | copy-start | bytes 147460
  51.1 150.3 %copy-start.7 = (f32[256]{0:T(256)S(1)}, f32[256]{0:T(256)}, u32[]{:S(2)}) copy-start(f32[256]{0:T(256)} %param.19) | copy-start | bytes 3076
  52.5 7.7 %collective-permute-start.1 = (f32[6,8,128]{2,1,0:T(8,128)S(1)}, f32[6,8,128]{2,1,0:T(8,128)S(1)}, u32[]{:S(2)}, u32[]{:S(2)}) collective-permute-start(f32[6,8,128]{2,1,0:T(8,128)S(1)} %constant_dynamic-slice_fusion.9), channel_id=1, source_target_pairs={{0,2},{1,3},{2,0},{3,1},{4,6},{5,7},{6,4},{7,5},{8,10},{9,11},{10,... | collective-permute-start | bytes 73736 | tf_op jit(solution)/shard_map/ppermute | solution.py:30
  55.4 157.5 %copy-start.3 = (s32[96,8]{1,0:T(8,128)}, s32[96,8]{1,0:T(8,128)S(1)}, u32[]{:S(2)}) copy-start(s32[96,8]{1,0:T(8,128)S(1)} %fusion.22) | copy-start | bytes 9220
  56.6 7.0 %collective-permute-start.2 = (f32[6,4]{1,0:T(8,128)S(1)}, f32[6,4]{1,0:T(8,128)S(1)}, u32[]{:S(2)}, u32[]{:S(2)}) collective-permute-start(f32[6,4]{1,0:T(8,128)S(1)} %constant_dynamic-slice_fusion.7), channel_id=1, source_target_pairs={{0,1},{1,0},{2,3},{3,2},{4,5},{5,4},{6,7},{7,6},{8,9},{9,8},{10,11... | collective-permute-start | bytes 296 | tf_op jit(solution)/shard_map/ppermute | solution.py:30
  59.9 5.1 %collective-permute-start.5 = (f32[6,4]{1,0:T(8,128)S(1)}, f32[6,4]{1,0:T(8,128)S(1)}, u32[]{:S(2)}, u32[]{:S(2)}) collective-permute-start(f32[6,4]{1,0:T(8,128)S(1)} %constant_dynamic-slice_fusion.2), channel_id=1, source_target_pairs={{0,1},{1,0},{2,3},{3,2},{4,5},{5,4},{6,7},{7,6},{8,9},{9,8},{10,11... | collective-permute-start | bytes 296 | tf_op jit(solution)/shard_map/ppermute | solution.py:30
  60.3 5.3 %collective-permute-start.3 = (f32[6,4,128]{2,1,0:T(4,128)S(1)}, f32[6,4,128]{2,1,0:T(4,128)S(1)}, u32[]{:S(2)}, u32[]{:S(2)}) collective-permute-start(f32[6,4,128]{2,1,0:T(4,128)S(1)} %constant_dynamic-slice_fusion.6), channel_id=1, source_target_pairs={{0,1},{1,0},{2,3},{3,2},{4,5},{5,4},{6,7},{7,6},{8,9},{9,8},{10,11... | collective-permute-start | bytes 36872 | tf_op jit(solution)/shard_map/ppermute | solution.py:30
  203.3 18.2 %all-to-all-start = ((bf16[16,1,24,256]{3,2,1,0:T(8,128)(2,1)}), bf16[16,1,24,256]{3,2,1,0:T(8,128)(2,1)}, u32[]{:S(2)}, u32[]{:S(2)}) async-start(bf16[16,1,24,256]{3,2,1,0:T(8,128)(2,1)} %bitcast.13), calls=%async_computation | async-start | bytes 393216 | tf_op jit(solution)/shard_map/all_to_all | solution.py:194
  212.9 3.4 %copy-start.4 = (f32[96,8]{0,1:T(8,128)S(1)}, f32[96,8]{0,1:T(8,128)}, u32[]{:S(2)}) copy-start(f32[96,8]{0,1:T(8,128)} %param.21) | copy-start | bytes 9220
  228.7 105.4 %copy-start.1 = (f32[96,256]{1,0:T(8,128)S(1)}, f32[96,256]{1,0:T(8,128)}, u32[]{:S(2)}) copy-start(f32[96,256]{1,0:T(8,128)} %all-reduce.3.cloned.1.call-done) | copy-start | bytes 294916
  230.6 13.3 %all-to-all-start.1 = ((bf16[1,24,16,256]{3,1,0,2:T(8,128)(2,1)}), bf16[1,24,16,256]{3,1,0,2:T(8,128)(2,1)S(1)}, u32[]{:S(2)}, u32[]{:S(2)}) async-start(bf16[1,24,16,256]{3,1,0,2:T(8,128)(2,1)} %fusion.4), calls=%async_computation.1 | async-start | bytes 393216 | tf_op jit(solution)/shard_map/all_to_all | solution.py:204
  235.3 98.7 %all-reduce.5.cloned.1.call-start = ((), (), s32[]{:S(2)}) async-start(), calls=%async_computation.3 | async-start | bytes 196608 | tf_op jit(solution)/shard_map/psum | solution.py:215
Sparse Core Ops, SparseCore 0:
  84.9 94.0 all-reduce.2
  244.8 89.1 all-reduce.4
where the time goes:
time: 343 us; the launch traced here: 342 us
  waiting for transfers between devices  196 us (57%)
  blocking collectives  73.9 us (22%)
  starting transfers between devices  23.4 us (7%)
  between operations  13.7 us (4%)
  local copies, waits for them, and re-layouts  13.3 us (4%)
  matrix products  12 us (3%)
  other arithmetic  10.2 us (3%)
    psum x1, waiting for transfers between devices, on_device(): projected = lax.psum(head_terms, ('sect', 'head'))  94.1 us
    psum x1, waiting for transfers between devices, on_device(): expert_mix = lax.psum(combined, ('sect', 'head'))  89.4 us
    all_gather x1, blocking collectives, on_device(): all_heads = lax.all_gather(queries, 'head', axis=1, tiled=True)  34.3 us
    psum x1, blocking collectives, on_device(): squares = lax.psum(jnp.sum(hidden_state * hidden_state, axis=1), 'batch')  21.5 us
    all_gather x1, blocking collectives, on_device(): lax.all_gather(attention, 'batch', axis=0, tiled=True)  18.2 us
    all_to_all x1, starting transfers between devices, on_device(): lax.all_to_all(outgoing, 'batch', split_axis=0, concat_axis=3, tiled=True)  9.58 us
    ppermute x6, starting transfers between devices, from_partner(): lax.ppermute(shard, axis, [(i, i ^ 1 << distance) for i in range(lax.axis...  9.03 us
  transfers between devices with their start and end apart: 10, of which 6 were waited for; matrix products, arithmetic and copies ran while one was open for 4% of the time, Pallas kernels for 0%

commit v1 on v0

--- a/solution.py
+++ b/solution.py
@@ -84,7 +84,9 @@
     local_pages = page_cache.shape[1]
     page_len = page_cache.shape[2]
     scaling = 1.0 / math.sqrt(head_dim)
-    all_heads = lax.all_gather(queries, "head", axis=1, tiled=True)
+    all_heads = jnp.concatenate(
+        lax.all_to_all(jnp.stack([queries] * lax.axis_size("head")), "head", 0, 0), axis=1
+    )
     kv_local = kv_index % (kv_heads // sect_size)
     group_query = lax.dynamic_slice_in_dim(all_heads, kv_local * head_dim, head_dim, 2)
     heads_dev = all_heads.shape[1] // group_size

time: 343 us -> 326 us (0.950)
  blocking collectives: 73.9 us -> 39.7 us
  starting transfers between devices: 23.4 us -> 32.1 us
  other arithmetic: 10.2 us -> 15.4 us
  local copies, waits for them, and re-layouts: 13.3 us -> 18 us
    all_gather x1 -> x0, blocking collectives: 34.3 us -> none  [on_device(): all_heads = lax.all_gather(queries, 'head', axis=1, tiled=True)]
    all_to_all x0 -> x1, starting transfers between devices: none -> 6.93 us  [on_device(): lax.all_to_all(jnp.stack([queries] * lax.axis_size('head')), 'head', 0, 0)]
  transfers between devices with their start and end apart: 10 -> 11, of which waited for: 6 -> 7; matrix products, arithmetic and copies ran while one was open for 4% -> 8% of each run, Pallas kernels for 0% -> 0%
where the time goes in v1:
time: 326 us; the launch traced here: 325 us
  waiting for transfers between devices  195 us (60%)
  blocking collectives  39.7 us (12%)
  starting transfers between devices  32.1 us (10%)
  local copies, waits for them, and re-layouts  18 us (6%)
  other arithmetic  15.4 us (5%)
  between operations  13.7 us (4%)
  matrix products  11.1 us (3%)
    psum x1, waiting for transfers between devices, on_device(): projected = lax.psum(head_terms, ('sect', 'head'))  92.6 us
    psum x1, waiting for transfers between devices, on_device(): expert_mix = lax.psum(combined, ('sect', 'head'))  89.4 us
    psum x1, blocking collectives, on_device(): squares = lax.psum(jnp.sum(hidden_state * hidden_state, axis=1), 'batch')  21.5 us
    all_gather x1, blocking collectives, on_device(): lax.all_gather(attention, 'batch', axis=0, tiled=True)  18.2 us
    ppermute x6, starting transfers between devices, from_partner(): lax.ppermute(shard, axis, [(i, i ^ 1 << distance) for i in range(lax.axis...  10.7 us
    all_to_all x1, starting transfers between devices, on_device(): lax.all_to_all(outgoing, 'batch', split_axis=0, concat_axis=3, tiled=True)  9.58 us
    all_to_all x1, starting transfers between devices, on_device(): lax.all_to_all(jnp.stack([queries] * lax.axis_size('head')), 'head', 0, 0)  6.93 us
  transfers between devices with their start and end apart: 11, of which 7 were waited for; matrix products, arithmetic and copies ran while one was open for 8% of the time, Pallas kernels for 0%

profile of v1, /device:TPU:32, one launch (start us, length us, event | category | flops | bytes accessed | tf_op | source)
XLA Modules:
  0.0 324.9 jit_solution(17558469268169185940)
XLA Ops:
  6.5 1.4 stack.2
  7.9 6.9 %all-to-all-start = ((bf16[8,6,2,256]{3,2,1,0:T(2,128)(2,1)}), bf16[8,6,2,256]{3,2,1,0:T(2,128)(2,1)S(1)}, u32[]{:S(2)}, u32[]{:S(2)}) async-start(bf16[8,6,2,256]{3,2,1,0:T(2,128)(2,1)} %stack.2), calls=%async_computation | async-start | bytes 98304 | tf_op jit(solution)/shard_map/all_to_all | solution.py:88
  14.9 0.8 copy.66
  15.7 0.1 eq.65
  15.8 0.1 eq.61
  15.9 0.7 constant_dynamic-slice_fusion.12
  16.6 0.6 slice_convert_fusion
  17.2 0.7 constant_dynamic-slice_fusion.13
  17.9 0.2 compare_reduce_fusion
  18.2 0.1 and.72
  18.3 0.1 and.73
  18.5 3.2 fusion.51
  21.7 0.7 fusion.16
  22.4 4.4 %reduce-window.6 = s32[64,6,128]{2,0,1:T(8,128)} reduce-window(s32[64,6,128]{2,0,1:T(8,128)} %fusion.16, s32[]{:T(128)} %constant.119.clone.1), window={size=1x1x128 pad=0_0x0_0x127_0}, to_apply=%region_4.5 | reduce-window | flops 6242304 | bytes 393220 | tf_op jit(solution)/shard_map/reduce-window
  26.8 1.2 slice_reduce_fusion
  28.0 1.1 fusion.13
  29.1 0.7 reduce_sum.49
  29.8 0.9 fusion.22
  30.7 0.1 compare_and_fusion
  30.8 0.5 copy-done.3
  31.3 0.8 fusion.2
  32.1 0.8 copy.75
  33.0 0.1 fusion.27
  33.1 0.6 fusion.52
  33.8 0.1 constant_dynamic-slice_fusion.10
  33.8 2.0 collective-permute-start
  35.8 0.9 fusion.8
  36.8 0.1 constant_dynamic-slice_fusion.4
  36.8 0.1 collective-permute-start.4
  36.9 1.1 convolution_add_fusion
  38.1 2.0 collective-permute-start.1
  40.1 0.4 collective-permute-done.4
  40.5 0.1 fusion.36
  40.6 3.0 collective-permute-start.2
  43.7 0.6 collective-permute-start.5
  44.2 0.1 multiply_add_fusion
  44.3 3.1 collective-permute-start.3
  47.4 1.4 collective-permute-done.5
  48.8 0.1 fusion.38
  48.9 0.8 collective-permute-done.3
  49.6 0.1 fusion.32
  49.7 18.2 %all-gather = bf16[16,6,512]{2,1,0:T(8,128)(2,1)S(1)} all-gather(bf16[1,6,512]{2,1,0:T(8,128)(2,1)S(1)} %reshape.192), channel_id=1, replica_groups=mesh['sect'=2,'batch'=16,'head'=8] {'batch'}, dimensions={0}, use_global_device_ids=true | all-gather | bytes 104448 | tf_op jit(solution)/shard_map/all_gather | solution.py:154
  68.0 0.8 fusion.53
  68.9 92.6 %all-reduce.3.cloned.1.call-done = f32[96,256]{1,0:T(8,128)} async-done(((f32[96,256]{1,0:T(8,128)}), f32[96,256]{1,0:T(8,128)}) %all-reduce.3.cloned.1.call-update) | async-done | bytes 98320 | tf_op jit(solution)/shard_map/psum | solution.py:158
  161.5 1.0 multiply_reduce_fusion
  162.5 21.5 %psum.22 = f32[96]{0:T(128)S(1)} all-reduce(f32[96]{0:T(128)S(1)} %multiply_reduce_fusion), channel_id=1, replica_groups=mesh['sect'=2,'batch'=16,'head'=8] {'batch'}, use_global_device_ids=true, to_apply=%region_11.12 | all-reduce | flops 96 | bytes 768 | tf_op jit(solution)/shard_map/psum | solution.py:160
  184.0 1.8 convolution_convert_fusion.1
  185.8 9.6 %all-to-all-start.1 = ((bf16[16,1,24,256]{3,2,1,0:T(8,128)(2,1)}), bf16[16,1,24,256]{3,2,1,0:T(8,128)(2,1)}, u32[]{:S(2)}, u32[]{:S(2)}) async-start(bf16[16,1,24,256]{3,2,1,0:T(8,128)(2,1)} %bitcast.14), calls=%async_computation.1 | async-start | bytes 393216 | tf_op jit(solution)/shard_map/all_to_all | solution.py:196
  195.4 3.4 %copy.83 = bf16[4096,384]{1,0:T(8,128)(2,1)S(1)} copy(bf16[4096,384]{0,1:T(8,128)(2,1)} %bitcast.93) | data formatting | bytes 6291456 | tf_op jit(solution)/shard_map/ecf,efd->ecd/dot_general | solution.py:201
  198.8 0.6 reduce_sum.50
  199.4 4.6 %all-to-all-done.1 = bf16[16,1,24,256]{3,2,1,0:T(8,128)(2,1)} async-done(((bf16[16,1,24,256]{3,2,1,0:T(8,128)(2,1)}), bf16[16,1,24,256]{3,2,1,0:T(8,128)(2,1)}, u32[]{:S(2)}, u32[]{:S(2)}) %all-to-all-start.1) | async-done | bytes 196640 | tf_op jit(solution)/shard_map/all_to_all | solution.py:196
  204.0 1.6 copy.77
  205.7 1.7 reshape.197
  207.4 3.8 %fusion.5 = f32[1,24,2,384]{3,1,2,0:T(8,128)S(1)} fusion(bf16[24,4096,1]{1,0,2:T(8,128)(2,1)} %reshape.197, bf16[4096,2,384]{2,1,0:T(2,128)(2,1)} %bitcast.104), kind=kOutput, calls=%fused_computation.10 | convolution fusion | flops 150994944 | bytes 6561792 | tf_op jit(solution)/shard_map/ecd,edgf->ecgf/dot_general | solution.py:197
  211.2 1.9 fusion.4
  213.1 4.8 %all-to-all-start.2 = ((bf16[1,24,16,256]{3,1,0,2:T(8,128)(2,1)}), bf16[1,24,16,256]{3,1,0,2:T(8,128)(2,1)S(1)}, u32[]{:S(2)}, u32[]{:S(2)}) async-start(bf16[1,24,16,256]{3,1,0,2:T(8,128)(2,1)} %fusion.4), calls=%async_computation.2 | async-start | bytes 393216 | tf_op jit(solution)/shard_map/all_to_all | solution.py:206
  217.9 0.7 broadcast_divide_fusion
  218.6 0.1 copy.73
  218.7 1.6 select_reduce_fusion
  220.3 0.2 copy.74
  220.5 5.8 %all-to-all-done.2 = bf16[1,24,16,256]{3,1,0,2:T(8,128)(2,1)S(1)} async-done(((bf16[1,24,16,256]{3,1,0,2:T(8,128)(2,1)}), bf16[1,24,16,256]{3,1,0,2:T(8,128)(2,1)S(1)}, u32[]{:S(2)}, u32[]{:S(2)}) %all-to-all-start.2) | async-done | bytes 196640 | tf_op jit(solution)/shard_map/all_to_all | solution.py:206
  226.3 0.8 fusion.54
  227.2 89.4 %all-reduce.5.cloned.1.call-done = f32[96,256]{1,0:T(8,128)} async-done(((f32[96,256]{1,0:T(8,128)}), f32[96,256]{1,0:T(8,128)}) %all-reduce.5.cloned.1.call-update) | async-done | bytes 98320 | tf_op jit(solution)/shard_map/psum | solution.py:217
  316.6 1.5 add_convert_fusion
  (44 shorter events, 0.7 us)
Async XLA Ops:
  6.5 61.4 %copy-start = (bf16[512,256]{1,0:T(8,128)(2,1)S(1)}, bf16[512,256]{1,0:T(8,128)(2,1)}, u32[]{:S(2)}) copy-start(bf16[512,256]{1,0:T(8,128)(2,1)} %param.17) | copy-start | bytes 786436
  7.9 25.0 %all-to-all-start = ((bf16[8,6,2,256]{3,2,1,0:T(2,128)(2,1)}), bf16[8,6,2,256]{3,2,1,0:T(2,128)(2,1)S(1)}, u32[]{:S(2)}, u32[]{:S(2)}) async-start(bf16[8,6,2,256]{3,2,1,0:T(2,128)(2,1)} %stack.2), calls=%async_computation | async-start | bytes 98304 | tf_op jit(solution)/shard_map/all_to_all | solution.py:88
  14.8 146.6 %all-reduce.3.cloned.1.call-start = ((), (), s32[]{:S(2)}) async-start(), calls=%async_computation.3 | async-start | bytes 196608 | tf_op jit(solution)/shard_map/psum | solution.py:158
  18.5 12.1 %copy-start.8 = (s32[6]{0:T(128)S(1)}, s32[6]{0:T(128)}, u32[]{:S(2)}) copy-start(s32[6]{0:T(128)} %param.15) | copy-start | bytes 76
  30.7 0.6 copy-start.3
  31.3 1.8 copy-start.5
  33.7 35.1 %copy-start.4 = (pred[768,96]{1,0:T(8,128)(4,1)S(1)}, pred[768,96]{1,0:T(8,128)(4,1)}, u32[]{:S(2)}) copy-start(pred[768,96]{1,0:T(8,128)(4,1)} %copy.75) | copy-start | bytes 221188
  33.7 127.7 %copy-start.2 = (bf16[96,256]{1,0:T(8,128)(2,1)S(1)}, bf16[96,256]{1,0:T(8,128)(2,1)}, u32[]{:S(2)}) copy-start(bf16[96,256]{1,0:T(8,128)(2,1)} %param.18) | copy-start | bytes 147460
  33.7 150.2 %copy-start.7 = (f32[256]{0:T(256)S(1)}, f32[256]{0:T(256)}, u32[]{:S(2)}) copy-start(f32[256]{0:T(256)} %param.19) | copy-start | bytes 3076
  33.8 6.2 %collective-permute-start = (f32[6,8]{1,0:T(8,128)S(1)}, f32[6,8]{1,0:T(8,128)S(1)}, u32[]{:S(2)}, u32[]{:S(2)}) collective-permute-start(f32[6,8]{1,0:T(8,128)S(1)} %constant_dynamic-slice_fusion.10), channel_id=1, source_target_pairs={{0,2},{1,3},{2,0},{3,1},{4,6},{5,7},{6,4},{7,5},{8,10},{9,11},{10,... | collective-permute-start | bytes 584 | tf_op jit(solution)/shard_map/ppermute | solution.py:30
  36.8 3.6 %collective-permute-start.4 = (f32[6,8]{1,0:T(8,128)S(1)}, f32[6,8]{1,0:T(8,128)S(1)}, u32[]{:S(2)}, u32[]{:S(2)}) collective-permute-start(f32[6,8]{1,0:T(8,128)S(1)} %constant_dynamic-slice_fusion.4), channel_id=1, source_target_pairs={{0,2},{1,3},{2,0},{3,1},{4,6},{5,7},{6,4},{7,5},{8,10},{9,11},{10,... | collective-permute-start | bytes 584 | tf_op jit(solution)/shard_map/ppermute | solution.py:30
  38.1 6.2 %collective-permute-start.1 = (f32[6,8,128]{2,1,0:T(8,128)S(1)}, f32[6,8,128]{2,1,0:T(8,128)S(1)}, u32[]{:S(2)}, u32[]{:S(2)}) collective-permute-start(f32[6,8,128]{2,1,0:T(8,128)S(1)} %constant_dynamic-slice_fusion.9), channel_id=1, source_target_pairs={{0,2},{1,3},{2,0},{3,1},{4,6},{5,7},{6,4},{7,5},{8,10},{9,11},{10,... | collective-permute-start | bytes 73736 | tf_op jit(solution)/shard_map/ppermute | solution.py:30
  40.6 6.8 %collective-permute-start.2 = (f32[6,4]{1,0:T(8,128)S(1)}, f32[6,4]{1,0:T(8,128)S(1)}, u32[]{:S(2)}, u32[]{:S(2)}) collective-permute-start(f32[6,4]{1,0:T(8,128)S(1)} %constant_dynamic-slice_fusion.7), channel_id=1, source_target_pairs={{0,1},{1,0},{2,3},{3,2},{4,5},{5,4},{6,7},{7,6},{8,9},{9,8},{10,11... | collective-permute-start | bytes 296 | tf_op jit(solution)/shard_map/ppermute | solution.py:30
  43.7 5.1 %collective-permute-start.5 = (f32[6,4]{1,0:T(8,128)S(1)}, f32[6,4]{1,0:T(8,128)S(1)}, u32[]{:S(2)}, u32[]{:S(2)}) collective-permute-start(f32[6,4]{1,0:T(8,128)S(1)} %constant_dynamic-slice_fusion.2), channel_id=1, source_target_pairs={{0,1},{1,0},{2,3},{3,2},{4,5},{5,4},{6,7},{7,6},{8,9},{9,8},{10,11... | collective-permute-start | bytes 296 | tf_op jit(solution)/shard_map/ppermute | solution.py:30
  44.3 5.3 %collective-permute-start.3 = (f32[6,4,128]{2,1,0:T(4,128)S(1)}, f32[6,4,128]{2,1,0:T(4,128)S(1)}, u32[]{:S(2)}, u32[]{:S(2)}) collective-permute-start(f32[6,4,128]{2,1,0:T(4,128)S(1)} %constant_dynamic-slice_fusion.6), channel_id=1, source_target_pairs={{0,1},{1,0},{2,3},{3,2},{4,5},{5,4},{6,7},{7,6},{8,9},{9,8},{10,11... | collective-permute-start | bytes 36872 | tf_op jit(solution)/shard_map/ppermute | solution.py:30
  185.8 18.2 %all-to-all-start.1 = ((bf16[16,1,24,256]{3,2,1,0:T(8,128)(2,1)}), bf16[16,1,24,256]{3,2,1,0:T(8,128)(2,1)}, u32[]{:S(2)}, u32[]{:S(2)}) async-start(bf16[16,1,24,256]{3,2,1,0:T(8,128)(2,1)} %bitcast.14), calls=%async_computation.1 | async-start | bytes 393216 | tf_op jit(solution)/shard_map/all_to_all | solution.py:196
  195.4 3.4 %copy-start.6 = (f32[96,8]{0,1:T(8,128)S(1)}, f32[96,8]{0,1:T(8,128)}, u32[]{:S(2)}) copy-start(f32[96,8]{0,1:T(8,128)} %param.21) | copy-start | bytes 9220
  211.2 105.4 %copy-start.1 = (f32[96,256]{1,0:T(8,128)S(1)}, f32[96,256]{1,0:T(8,128)}, u32[]{:S(2)}) copy-start(f32[96,256]{1,0:T(8,128)} %all-reduce.3.cloned.1.call-done) | copy-start | bytes 294916
  213.1 13.3 %all-to-all-start.2 = ((bf16[1,24,16,256]{3,1,0,2:T(8,128)(2,1)}), bf16[1,24,16,256]{3,1,0,2:T(8,128)(2,1)S(1)}, u32[]{:S(2)}, u32[]{:S(2)}) async-start(bf16[1,24,16,256]{3,1,0,2:T(8,128)(2,1)} %fusion.4), calls=%async_computation.2 | async-start | bytes 393216 | tf_op jit(solution)/shard_map/all_to_all | solution.py:206
  217.8 98.7 %all-reduce.5.cloned.1.call-start = ((), (), s32[]{:S(2)}) async-start(), calls=%async_computation.4 | async-start | bytes 196608 | tf_op jit(solution)/shard_map/psum | solution.py:217
Sparse Core Ops, SparseCore 0:
  69.0 92.4 all-reduce.2
  227.3 89.1 all-reduce.4
